TPU v7x, 512 devices: a whole 4x4x16 slice. The times are simulated.
512 devices in a mesh: lat: 32 (over z, core), lon: 16 (over x, y).
Axes of the slice: x: 4, y: 4, z: 16, core: 2. Of those that a mesh axis runs over, the one named last changes fastest.
Arguments:
- source: float32 [8, 1024, 2048], P(None, 'lat', 'lon'), may hold values from -6 to 6
- kappa_lon: bfloat16 [8, 1024, 2048], P(None, 'lat', 'lon'), may hold values from 32768 to 262144
- kappa_lat: bfloat16 [8, 1024, 2048], P(None, 'lat', 'lon'), may hold values from 2048 to 16384
- sea_mask: int32 [8, 1024, 2048], P(None, 'lat', 'lon'), may hold values 0 or 1
Outputs:
- analysis: float32 [8, 1024, 2048], P(None, 'lat', 'lon')
All inputs are finite; a program needn't handle non-finite values. No bound on the sum of `sea_mask` on one device may be relied on, other than what follows from the above.
Results may differ from a plain program's by a relative error of at most 0.0003.
Values sent between devices are 32-bit elements; how exact they have to be, the bound alone decides.
No kernel may reach another device: no remote copies, remote signals or barrier semaphores. Data moves between devices by JAX's collectives and lax.ppermute only.
A program may use at most 64 MiB of HBM per device.

v0:
```python
import jax
import jax.numpy as jnp
from jax import lax
from jax.sharding import PartitionSpec as P


def padded(array, sides, width):
    for axis, dim in sides:
        peers, length = (lax.axis_size(axis), array.shape[dim])
        up = [(i, (i + 1) % peers) for i in range(peers)]
        down = [(j, i) for i, j in up]
        last = lax.slice_in_dim(array, length - width, length, axis=dim)
        leading = lax.slice_in_dim(array, 0, width, axis=dim)
        before = lax.ppermute(last, axis, up)
        after = lax.ppermute(leading, axis, down)
        array = jnp.concatenate([before, array, after], axis=dim)
    return array


def earlier(values, stride, axis):
    length = values.shape[axis]
    padding = jnp.zeros_like(lax.slice_in_dim(values, 0, stride, axis=axis))
    return jnp.concatenate([padding, lax.slice_in_dim(values, 0, length - stride, axis=axis)], axis)


def following(values, stride, axis):
    length = values.shape[axis]
    padding = jnp.zeros_like(lax.slice_in_dim(values, 0, stride, axis=axis))
    return jnp.concatenate([lax.slice_in_dim(values, stride, length, axis=axis), padding], axis)


def local_solve(lower_band, upper_band, excess, sources, axis):
    length = lower_band.shape[axis]
    stride = 1
    while stride < length:
        inverse = 1.0 / (excess - lower_band - upper_band)
        left_weight = -lower_band * earlier(inverse, stride, axis)
        right_coefficient = -upper_band * following(inverse, stride, axis)
        new_lower = left_weight * earlier(lower_band, stride, axis)
        new_upper = right_coefficient * following(upper_band, stride, axis)
        excess = (
            excess
            + left_weight * earlier(excess, stride, axis)
            + right_coefficient * following(excess, stride, axis)
        )
        sources = (
            sources
            + left_weight * earlier(sources, stride, axis + 1)
            + right_coefficient * following(sources, stride, axis + 1)
        )
        lower_band, upper_band = (new_lower, new_upper)
        stride = stride * 2
    return sources / (excess - lower_band - upper_band)


def reduced_from(own_terms, next_terms):
    coupling, own_source, own_excess, upper_end = own_terms
    next_particular, next_right, next_deficit = next_terms
    return (
        coupling,
        upper_end * next_right,
        own_excess - upper_end * next_deficit,
        own_source - upper_end * next_particular,
    )


def parallel_cyclic_reduction_update(tridiagonal_system, leading_terms, trailing_terms):
    lower_band, upper_band, excess, sources = tridiagonal_system
    lower_b, upper_b, excess_b, source_b = leading_terms
    lower_a, upper_a, excess_a, source_a = trailing_terms
    left_weight = -lower_band / (excess_b - lower_b - upper_b)
    right_coefficient = -upper_band / (excess_a - lower_a - upper_a)
    return (
        left_weight * lower_b,
        right_coefficient * upper_a,
        excess + left_weight * excess_b + right_coefficient * excess_a,
        sources + left_weight * source_b + right_coefficient * source_a,
    )


def circular_solve(tridiagonal_system):
    devices = tridiagonal_system[0].shape[0]
    stride = 1
    while stride < devices:
        leading_terms = tuple(
            (jnp.roll(ensemble_member, stride, 0) for ensemble_member in tridiagonal_system)
        )
        trailing_terms = tuple(
            (jnp.roll(ensemble_member, -stride, 0) for ensemble_member in tridiagonal_system)
        )
        tridiagonal_system = parallel_cyclic_reduction_update(
            tridiagonal_system, leading_terms, trailing_terms
        )
        stride = stride * 2
    return tridiagonal_system[3] / tridiagonal_system[2]


def gathered_solve(gathered, device_index):
    own_terms = gathered[:4]
    next_terms = tuple((jnp.roll(ensemble_member, -1, 0) for ensemble_member in gathered[4:]))
    interface = circular_solve(reduced_from(own_terms, next_terms))
    devices = interface.shape[0]
    here_value = lax.dynamic_index_in_dim(interface, device_index, 0, keepdims=False)
    before_value = lax.dynamic_index_in_dim(
        interface, (device_index + devices - 1) % devices, 0, keepdims=False
    )
    return (before_value, here_value)


def lon_gathered(own_terms, head_terms):
    gathered = (
        lax.all_gather(own_terms[0][None], "lon", axis=0, tiled=True),
        lax.all_gather(own_terms[1][None], "lon", axis=0, tiled=True),
        lax.all_gather(own_terms[2][None], "lon", axis=0, tiled=True),
        lax.all_gather(own_terms[3][None], "lon", axis=0, tiled=True),
        lax.all_gather(head_terms[0][None], "lon", axis=0, tiled=True),
        lax.all_gather(head_terms[1][None], "lon", axis=0, tiled=True),
        lax.all_gather(head_terms[2][None], "lon", axis=0, tiled=True),
    )
    return gathered_solve(gathered, lax.axis_index("lon"))


def lat_gathered(own_terms, head_terms):
    gathered = (
        lax.all_gather(own_terms[0][None], "lat", axis=0, tiled=True),
        lax.all_gather(own_terms[1][None], "lat", axis=0, tiled=True),
        lax.all_gather(own_terms[2][None], "lat", axis=0, tiled=True),
        lax.all_gather(own_terms[3][None], "lat", axis=0, tiled=True),
        lax.all_gather(head_terms[0][None], "lat", axis=0, tiled=True),
        lax.all_gather(head_terms[1][None], "lat", axis=0, tiled=True),
        lax.all_gather(head_terms[2][None], "lat", axis=0, tiled=True),
    )
    return gathered_solve(gathered, lax.axis_index("lat"))


def line_pass(values, left_face, right_face, axis, reduce_edges):
    length = values.shape[axis]
    position = lax.broadcasted_iota(jnp.int32, values.shape, axis)
    is_first = position == 0
    is_last = position == length - 1
    is_penult = position == length - 2
    lower_band = jnp.where(is_first | is_last, 0.0, -left_face)
    upper_band = jnp.where(is_penult | is_last, 0.0, -right_face)
    excess = 1.0 + jnp.where(is_first, left_face, 0.0) + jnp.where(is_penult, right_face, 0.0)
    sources = jnp.stack(
        [
            jnp.where(is_last, 0.0, values),
            jnp.where(is_first, left_face, 0.0),
            jnp.where(is_penult, right_face, 0.0) + jnp.where(is_last, 1.0, 0.0),
            jnp.where(is_last, 0.0, 1.0),
        ],
        0,
    )
    solved = local_solve(lower_band, upper_band, excess, sources, axis)
    particular, from_left, right_contribution, deficit = (
        solved[0],
        solved[1],
        solved[2],
        solved[3],
    )

    def row_at(ensemble_member, place):
        return lax.index_in_dim(ensemble_member, place, axis, keepdims=False)

    lower_end = -row_at(left_face, length - 1)
    upper_end = -row_at(right_face, length - 1)
    own_terms = (
        lower_end * row_at(from_left, length - 2),
        row_at(values, length - 1) - lower_end * row_at(particular, length - 2),
        1.0 - lower_end * row_at(deficit, length - 2),
        upper_end,
    )
    head_terms = (row_at(particular, 0), row_at(right_contribution, 0), row_at(deficit, 0))
    before_value, here_value = reduce_edges(own_terms, head_terms)
    return (
        particular
        + from_left * jnp.expand_dims(before_value, axis)
        + right_contribution * jnp.expand_dims(here_value, axis)
    )


def shards(source, kappa_lon, kappa_lat, sea_mask):
    wet_cells = sea_mask.astype(jnp.float32)
    lon_kappa = kappa_lon.astype(jnp.float32)
    lat_kappa = kappa_lat.astype(jnp.float32)
    wet_pad, lon_pad, lat_pad = (
        padded(wet_cells, (("lat", 1), ("lon", 2)), 1),
        padded(lon_kappa, (("lat", 1), ("lon", 2)), 1),
        padded(lat_kappa, (("lat", 1), ("lon", 2)), 1),
    )
    lon_wet = wet_pad[:, 1:-1, :]
    lon_faces = lon_pad[:, 1:-1, :-1] * lon_wet[:, :, :-1] * lon_wet[:, :, 1:]
    lon_pass = line_pass(source, lon_faces[:, :, :-1], lon_faces[:, :, 1:], 2, lon_gathered)
    lat_wet = wet_pad[:, :, 1:-1]
    lat_faces = lat_pad[:, :-1, 1:-1] * lat_wet[:, :-1, :] * lat_wet[:, 1:, :]
    device_index = lax.axis_index("lat")
    devices = lax.axis_size("lat")
    position = lax.broadcasted_iota(jnp.int32, lat_faces.shape, 1)
    outer_face = (position == 0) & (device_index == 0) | (position == lat_faces.shape[1] - 1) & (
        device_index == devices - 1
    )
    lat_faces = jnp.where(outer_face, 0.0, lat_faces)
    lat_pass = line_pass(lon_pass, lat_faces[:, :-1, :], lat_faces[:, 1:, :], 1, lat_gathered)
    return wet_cells * 4.0 * jnp.sqrt(jnp.sqrt(lon_kappa * lat_kappa)) * lat_pass


def solution(mesh):
    return jax.shard_map(
        shards,
        mesh=mesh,
        in_specs=(
            P(None, "lat", "lon"),
            P(None, "lat", "lon"),
            P(None, "lat", "lon"),
            P(None, "lat", "lon"),
        ),
        out_specs=P(None, "lat", "lon"),
        check_vma=False,
    )
```

profile of v0, /device:TPU:1, one launch (start us, length us, event | category | flops | bytes accessed | tf_op | source)
XLA Modules:
  0.0 489.6 jit_solution(17990874060258347863)
XLA Ops:
  0.0 0.9 copy_convert_fusion.1
  0.9 3.0 collective-permute-start.7
  3.9 1.0 copy_convert_fusion
  4.9 3.8 collective-permute-start.4
  8.8 0.9 copy_convert_fusion.2
  9.7 3.6 collective-permute-start.1
  14.4 1.0 fusion.143
  15.6 6.8 %collective-permute-start.6 = (f32[8,34,1]{2,0,1:T(8,128)S(1)}, f32[8,34,1]{2,0,1:T(8,128)S(1)}, u32[]{:S(2)}, u32[]{:S(2)}) collective-permute-start(f32[8,34,1]{2,0,1:T(8,128)S(1)} %get-tuple-element.145), channel_id=1, source_target_pairs={{1,0},{2,1},{3,2},{4,3},{5,4},{6,5},{7,6},{8,7},{9,8},{10,9},{11,1... | collective-permute-start | bytes 3272 | tf_op jit(solution)/shard_map/ppermute | solution.py:15
  22.5 1.9 collective-permute-start.5
  24.5 1.9 collective-permute-start.2
  26.9 0.8 subtract_divide_fusion.3
  27.8 0.8 subtract_divide_fusion.2
  28.7 0.8 subtract_divide_fusion.1
  30.4 0.8 multiply_subtract_fusion
  31.1 0.8 collective-permute-done.5
  32.0 3.5 collective-permute-done.2
  42.4 0.9 fusion.4
  43.3 26.5 %all-gather.5 = f32[128,32,1]{2,0,1:T(8,128)S(1)} all-gather(f32[8,32,1]{2,0,1:T(8,128)S(1)} %get-tuple-element.263), channel_id=7, replica_groups=mesh['lat'=32,'lon'=16] {'lon'}, dimensions={0}, use_global_device_ids=true | all-gather | bytes 17408 | tf_op jit(solution)/shard_map/all_gather | solution.py:118
  69.8 1.4 copy-done
  71.2 24.5 %all-gather.6 = f32[128,32,1]{2,0,1:T(8,128)S(1)} all-gather(f32[8,32,1]{2,0,1:T(8,128)S(1)} %bitcast.109), channel_id=8, replica_groups=mesh['lat'=32,'lon'=16] {'lon'}, dimensions={0}, use_global_device_ids=true | all-gather | bytes 17408 | tf_op jit(solution)/shard_map/all_gather | solution.py:117
  95.7 1.4 copy-done.1
  97.0 23.1 %all-gather.2 = f32[128,32,1]{2,0,1:T(8,128)S(1)} all-gather(f32[8,32,1]{2,0,1:T(8,128)S(1)} %get-tuple-element.153), channel_id=4, replica_groups=mesh['lat'=32,'lon'=16] {'lon'}, dimensions={0}, use_global_device_ids=true | all-gather | bytes 17408 | tf_op jit(solution)/shard_map/all_gather | solution.py:116
  120.8 1.5 slice.1270
  123.0 1.4 copy.166
  124.4 22.4 %all-gather.4 = f32[128,32,1]{2,0,1:T(8,128)S(1)} all-gather(f32[8,32,1]{2,0,1:T(8,128)S(1)} %get-tuple-element.140), channel_id=6, replica_groups=mesh['lat'=32,'lon'=16] {'lon'}, dimensions={0}, use_global_device_ids=true | all-gather | bytes 17408 | tf_op jit(solution)/shard_map/all_gather | solution.py:114
  146.9 1.1 copy.165
  148.0 25.6 %all-gather.1 = f32[128,32,1]{2,0,1:T(8,128)} all-gather(f32[8,32,1]{2,0,1:T(8,128)S(1)} %get-tuple-element.142), channel_id=3, replica_groups=mesh['lat'=32,'lon'=16] {'lon'}, dimensions={0}, use_global_device_ids=true | all-gather | bytes 17408 | tf_op jit(solution)/shard_map/all_gather | solution.py:115
  173.7 2.6 copy.161
  176.4 1.4 copy.170
  178.0 2.9 copy.162
  180.9 24.8 %all-gather = f32[128,32,1]{2,0,1:T(8,128)S(1)} all-gather(f32[8,32,1]{2,0,1:T(8,128)S(1)} %get-tuple-element.143), channel_id=2, replica_groups=mesh['lat'=32,'lon'=16] {'lon'}, dimensions={0}, use_global_device_ids=true | all-gather | bytes 17408 | tf_op jit(solution)/shard_map/all_gather | solution.py:113
  205.8 1.1 copy.160
  206.9 0.9 fusion.40
  209.7 29.7 %all-gather.3 = f32[128,32,1]{2,0,1:T(8,128)S(1)} all-gather(f32[8,32,1]{2,0,1:T(8,128)} %get-tuple-element.141), channel_id=5, replica_groups=mesh['lat'=32,'lon'=16] {'lon'}, dimensions={0}, use_global_device_ids=true | all-gather | bytes 17408 | tf_op jit(solution)/shard_map/all_gather | solution.py:112
  239.4 2.2 fusion.84
  243.1 2.3 copy.169
  245.4 1.0 copy.168
  246.5 1.7 copy.164
  248.2 1.1 copy.173
  249.3 2.3 copy.172
  255.8 0.8 fusion.63
  256.6 61.3 %all-gather.12 = f32[256,1,128]{2,0,1:T(8,128)S(1)} all-gather(f32[8,1,128]{2,0,1:T(8,128)S(1)} %get-tuple-element.238), channel_id=14, replica_groups=mesh['lat'=32,'lon'=16] {'lat'}, dimensions={0}, use_global_device_ids=true | all-gather | bytes 135168 | tf_op jit(solution)/shard_map/all_gather | solution.py:131
  317.9 27.5 %all-gather.13 = f32[256,1,128]{2,0,1:T(8,128)S(1)} all-gather(f32[8,1,128]{2,0,1:T(8,128)S(1)} %slice.1405), channel_id=15, replica_groups=mesh['lat'=32,'lon'=16] {'lat'}, dimensions={0}, use_global_device_ids=true | all-gather | bytes 135168 | tf_op jit(solution)/shard_map/all_gather | solution.py:130
  345.4 28.8 %all-gather.9 = f32[256,1,128]{2,0,1:T(8,128)S(1)} all-gather(f32[8,1,128]{2,0,1:T(8,128)S(1)} %get-tuple-element.152), channel_id=11, replica_groups=mesh['lat'=32,'lon'=16] {'lat'}, dimensions={0}, use_global_device_ids=true | all-gather | bytes 135168 | tf_op jit(solution)/shard_map/all_gather | solution.py:129
  374.2 27.5 %all-gather.11 = f32[256,1,128]{2,0,1:T(8,128)S(1)} all-gather(f32[8,1,128]{2,0,1:T(8,128)S(1)} %get-tuple-element.148), channel_id=13, replica_groups=mesh['lat'=32,'lon'=16] {'lat'}, dimensions={0}, use_global_device_ids=true | all-gather | bytes 135168 | tf_op jit(solution)/shard_map/all_gather | solution.py:127
  401.6 28.8 %all-gather.8 = f32[256,1,128]{2,0,1:T(8,128)S(1)} all-gather(f32[8,1,128]{2,0,1:T(8,128)S(1)} %get-tuple-element.150), channel_id=10, replica_groups=mesh['lat'=32,'lon'=16] {'lat'}, dimensions={0}, use_global_device_ids=true | all-gather | bytes 135168 | tf_op jit(solution)/shard_map/all_gather | solution.py:128
  430.4 27.4 %all-gather.7 = f32[256,1,128]{2,0,1:T(8,128)S(1)} all-gather(f32[8,1,128]{2,0,1:T(8,128)S(1)} %get-tuple-element.151), channel_id=9, replica_groups=mesh['lat'=32,'lon'=16] {'lat'}, dimensions={0}, use_global_device_ids=true | all-gather | bytes 135168 | tf_op jit(solution)/shard_map/all_gather | solution.py:126
  457.9 28.8 %all-gather.10 = f32[256,1,128]{2,0,1:T(8,128)S(1)} all-gather(f32[8,1,128]{2,0,1:T(8,128)S(1)} %get-tuple-element.149), channel_id=12, replica_groups=mesh['lat'=32,'lon'=16] {'lat'}, dimensions={0}, use_global_device_ids=true | all-gather | bytes 135168 | tf_op jit(solution)/shard_map/all_gather | solution.py:125
  (271 shorter events, 20.9 us)
Async XLA Ops:
  0.9 25.6 %collective-permute-start.7 = (f32[8,1,128]{2,0,1:T(8,128)S(1)}, f32[8,1,128]{2,0,1:T(8,128)S(1)}, u32[]{:S(2)}, u32[]{:S(2)}) collective-permute-start(f32[8,1,128]{2,0,1:T(8,128)S(1)} %slice.1338), channel_id=1, source_target_pairs={{0,16},{16,32},{32,48},{48,64},{64,80},{80,96},{96,112},{112,128},... | collective-permute-start | bytes 12296 | tf_op jit(solution)/shard_map/ppermute | solution.py:14
  4.9 10.6 %collective-permute-start.3 = (f32[8,1,128]{2,0,1:T(8,128)S(1)}, f32[8,1,128]{2,0,1:T(8,128)S(1)}, u32[]{:S(2)}, u32[]{:S(2)}) collective-permute-start(f32[8,1,128]{2,0,1:T(8,128)S(1)} %get-tuple-element.297), channel_id=1, source_target_pairs={{0,16},{16,32},{32,48},{48,64},{64,80},{80,96},{96,112},{112,128},... | collective-permute-start | bytes 12296 | tf_op jit(solution)/shard_map/ppermute | solution.py:14
  4.9 10.6 %collective-permute-start.4 = (f32[8,1,128]{2,0,1:T(8,128)S(1)}, f32[8,1,128]{2,0,1:T(8,128)S(1)}, u32[]{:S(2)}, u32[]{:S(2)}) collective-permute-start(f32[8,1,128]{2,0,1:T(8,128)S(1)} %get-tuple-element.296), channel_id=1, source_target_pairs={{16,0},{32,16},{48,32},{64,48},{80,64},{96,80},{112,96},{128,112},... | collective-permute-start | bytes 12296 | tf_op jit(solution)/shard_map/ppermute | solution.py:15
  9.7 14.7 %collective-permute-start.1 = (f32[8,1,128]{2,0,1:T(8,128)S(1)}, f32[8,1,128]{2,0,1:T(8,128)S(1)}, u32[]{:S(2)}, u32[]{:S(2)}) collective-permute-start(f32[8,1,128]{2,0,1:T(8,128)S(1)} %get-tuple-element.295), channel_id=1, source_target_pairs={{16,0},{32,16},{48,32},{64,48},{80,64},{96,80},{112,96},{128,112},... | collective-permute-start | bytes 12296 | tf_op jit(solution)/shard_map/ppermute | solution.py:15
  13.3 11.2 %collective-permute-start = (f32[8,1,128]{2,0,1:T(8,128)S(1)}, f32[8,1,128]{2,0,1:T(8,128)S(1)}, u32[]{:S(2)}, u32[]{:S(2)}) collective-permute-start(f32[8,1,128]{2,0,1:T(8,128)S(1)} %get-tuple-element.294), channel_id=1, source_target_pairs={{0,16},{16,32},{32,48},{48,64},{64,80},{80,96},{96,112},{112,128},... | collective-permute-start | bytes 12296 | tf_op jit(solution)/shard_map/ppermute | solution.py:14
  15.6 15.5 %collective-permute-start.6 = (f32[8,34,1]{2,0,1:T(8,128)S(1)}, f32[8,34,1]{2,0,1:T(8,128)S(1)}, u32[]{:S(2)}, u32[]{:S(2)}) collective-permute-start(f32[8,34,1]{2,0,1:T(8,128)S(1)} %get-tuple-element.145), channel_id=1, source_target_pairs={{1,0},{2,1},{3,2},{4,3},{5,4},{6,5},{7,6},{8,7},{9,8},{10,9},{11,1... | collective-permute-start | bytes 3272 | tf_op jit(solution)/shard_map/ppermute | solution.py:15
  22.5 9.5 %collective-permute-start.5 = (f32[8,34,1]{2,0,1:T(8,128)S(1)}, f32[8,34,1]{2,0,1:T(8,128)S(1)}, u32[]{:S(2)}, u32[]{:S(2)}) collective-permute-start(f32[8,34,1]{2,0,1:T(8,128)S(1)} %get-tuple-element.144), channel_id=1, source_target_pairs={{0,1},{1,2},{2,3},{3,4},{4,5},{5,6},{6,7},{7,8},{8,9},{9,10},{10,1... | collective-permute-start | bytes 3272 | tf_op jit(solution)/shard_map/ppermute | solution.py:14
  24.5 10.9 %collective-permute-start.2 = (f32[8,34,1]{2,0,1:T(8,128)S(1)}, f32[8,34,1]{2,0,1:T(8,128)S(1)}, u32[]{:S(2)}, u32[]{:S(2)}) collective-permute-start(f32[8,34,1]{2,0,1:T(8,128)S(1)} %pad_maximum_fusion.11), channel_id=1, source_target_pairs={{0,1},{1,2},{2,3},{3,4},{4,5},{5,6},{6,7},{7,8},{8,9},{9,10},{10,1... | collective-permute-start | bytes 3272 | tf_op jit(solution)/shard_map/ppermute | solution.py:14
  42.3 0.9 copy-start.3
  42.4 28.8 %copy-start.4 = (f32[8,32,128]{2,0,1:T(8,128)}, f32[8,32,128]{2,0,1:T(8,128)S(1)}, u32[]{:S(2)}) copy-start(f32[8,32,128]{2,0,1:T(8,128)S(1)} %get-tuple-element.121) | copy-start | bytes 393220
  69.8 1.4 copy-start
  95.7 1.4 copy-start.1
  120.1 2.2 slice-start
  120.8 2.3 slice-start.1
  148.0 28.3 %slice-start.2 = ((f32[128,32,1]{2,0,1:T(8,128)}), f32[8,32,1]{2,0,1:T(8,128)S(1)}, s32[]{:S(2)}) async-start(f32[128,32,1]{2,0,1:T(8,128)} %copy-done.1), calls=%async_computation.2 | async-start | bytes 262144 | tf_op jit(solution)/shard_map/jit(_roll_static)/slice | solution.py:100
  148.0 28.4 %slice-start.3 = ((f32[128,32,1]{2,0,1:T(8,128)}), f32[120,32,1]{2,0,1:T(8,128)S(1)}, s32[]{:S(2)}) async-start(f32[128,32,1]{2,0,1:T(8,128)} %copy-done.1), calls=%async_computation.3 | async-start | bytes 3932160 | tf_op jit(solution)/shard_map/jit(_roll_static)/slice | solution.py:100
  173.7 4.2 copy-start.10
  248.2 3.4 copy-start.2
  248.2 3.4 copy-start.18
  248.2 3.4 copy-start.21
  248.2 3.4 copy-start.22
  248.2 3.4 copy-start.23
  248.2 3.4 copy-start.24
  252.0 0.6 copy-start.26
  252.1 0.8 copy-start.25
  252.3 0.9 copy-start.11
  252.4 1.0 copy-start.12
  253.3 0.9 copy-start.13
  253.3 1.0 copy-start.14
  253.5 1.0 copy-start.5
  253.5 1.0 copy-start.6
  254.4 0.9 copy-start.7
  254.5 1.0 copy-start.8
  254.6 1.0 copy-start.15
  254.6 1.0 copy-start.16
  254.6 1.0 copy-start.17
  487.8 0.9 copy-start.9
  487.8 0.9 copy-start.19
  487.8 0.9 copy-start.20
where the time goes:
time: 490 us
  blocking collectives  407 us (83%)
  local copies, waits for them, and re-layouts  38.8 us (8%)
  starting transfers between devices  21.2 us (4%)
  other arithmetic  17.1 us (3%)
    all_gather x1, blocking collectives, lat_gathered(): lax.all_gather(head_terms[2][None], 'lat', axis=0, tiled=True)  61.3 us
    all_gather x1, blocking collectives, lon_gathered(): lax.all_gather(own_terms[0][None], 'lon', axis=0, tiled=True)  29.7 us
    all_gather x1, blocking collectives, lat_gathered(): lax.all_gather(head_terms[0][None], 'lat', axis=0, tiled=True)  28.8 us
    all_gather x1, blocking collectives, lat_gathered(): lax.all_gather(own_terms[0][None], 'lat', axis=0, tiled=True)  28.8 us
    all_gather x1, blocking collectives, lat_gathered(): lax.all_gather(own_terms[3][None], 'lat', axis=0, tiled=True)  28.8 us
    all_gather x1, blocking collectives, lat_gathered(): lax.all_gather(own_terms[2][None], 'lat', axis=0, tiled=True)  27.5 us
    all_gather x1, blocking collectives, lat_gathered(): lax.all_gather(head_terms[1][None], 'lat', axis=0, tiled=True)  27.5 us
    all_gather x1, blocking collectives, lat_gathered(): lax.all_gather(own_terms[1][None], 'lat', axis=0, tiled=True)  27.4 us
  transfers between devices with their start and end apart: 8, of which 2 were waited for; matrix products, arithmetic and copies ran while one was open for 2% of the time, Pallas kernels for 0%

commit v1 on v0

--- a/solution.py
+++ b/solution.py
@@ -2,6 +2,11 @@
 import jax.numpy as jnp
 from jax import lax
 from jax.sharding import PartitionSpec as P
+
+
+def all_by_exchange(shard, axis, dim):
+    sent = jnp.stack([shard] * lax.axis_size(axis))
+    return jnp.concatenate(lax.all_to_all(sent, axis, 0, 0), axis=dim)
 
 
 def padded(array, sides, width):
@@ -127,7 +132,7 @@
         lax.all_gather(own_terms[2][None], "lat", axis=0, tiled=True),
         lax.all_gather(own_terms[3][None], "lat", axis=0, tiled=True),
         lax.all_gather(head_terms[0][None], "lat", axis=0, tiled=True),
-        lax.all_gather(head_terms[1][None], "lat", axis=0, tiled=True),
+        all_by_exchange(head_terms[1][None], "lat", 0),
         lax.all_gather(head_terms[2][None], "lat", axis=0, tiled=True),
     )
     return gathered_solve(gathered, lax.axis_index("lat"))

time: 490 us -> 476 us (0.971)
  blocking collectives: 407 us -> 385 us
  starting transfers between devices: 21.2 us -> 27.5 us
    all_gather x1 -> x0, blocking collectives: 27.5 us -> none  [lat_gathered(): lax.all_gather(head_terms[1][None], 'lat', axis=0, tiled=True)]
    all_to_all x0 -> x1, starting transfers between devices: none -> 6.33 us  [all_by_exchange(): return jnp.concatenate(lax.all_to_all(sent, axis, 0, 0), axis=dim)]
  transfers between devices with their start and end apart: 8 -> 9, of which waited for: 2 -> 2; matrix products, arithmetic and copies ran while one was open for 2% -> 2% of each run, Pallas kernels for 0% -> 0%
where the time goes in v1:
time: 476 us; the launch traced here: 475 us
  blocking collectives  385 us (81%)
  local copies, waits for them, and re-layouts  39.5 us (8%)
  starting transfers between devices  27.5 us (6%)
  other arithmetic  17.1 us (4%)
    all_gather x1, blocking collectives, lat_gathered(): lax.all_gather(head_terms[2][None], 'lat', axis=0, tiled=True)  61.4 us
    all_gather x1, blocking collectives, lat_gathered(): lax.all_gather(head_terms[0][None], 'lat', axis=0, tiled=True)  33.2 us
    all_gather x1, blocking collectives, lon_gathered(): lax.all_gather(own_terms[0][None], 'lon', axis=0, tiled=True)  29.7 us
    all_gather x1, blocking collectives, lat_gathered(): lax.all_gather(own_terms[1][None], 'lat', axis=0, tiled=True)  29.5 us
    all_gather x1, blocking collectives, lat_gathered(): lax.all_gather(own_terms[3][None], 'lat', axis=0, tiled=True)  28.8 us
    all_gather x1, blocking collectives, lat_gathered(): lax.all_gather(own_terms[0][None], 'lat', axis=0, tiled=True)  27.9 us
    all_gather x1, blocking collectives, lat_gathered(): lax.all_gather(own_terms[2][None], 'lat', axis=0, tiled=True)  27.5 us
    all_gather x1, blocking collectives, lon_gathered(): lax.all_gather(head_terms[2][None], 'lon', axis=0, tiled=True)  26.5 us
  transfers between devices with their start and end apart: 9, of which 2 were waited for; matrix products, arithmetic and copies ran while one was open for 2% of the time, Pallas kernels for 0%

profile of v1, /device:TPU:1, one launch (start us, length us, event | category | flops | bytes accessed | tf_op | source)
XLA Modules:
  0.0 474.9 jit_solution(16520644863435975400)
XLA Ops:
  0.0 0.9 copy_convert_fusion.1
  0.9 3.0 collective-permute-start.7
  3.9 1.0 copy_convert_fusion
  4.9 3.8 collective-permute-start.4
  8.8 0.9 copy_convert_fusion.2
  9.7 3.6 collective-permute-start.1
  14.4 1.0 fusion.143
  15.6 6.8 %collective-permute-start.6 = (f32[8,34,1]{2,0,1:T(8,128)S(1)}, f32[8,34,1]{2,0,1:T(8,128)S(1)}, u32[]{:S(2)}, u32[]{:S(2)}) collective-permute-start(f32[8,34,1]{2,0,1:T(8,128)S(1)} %get-tuple-element.145), channel_id=1, source_target_pairs={{1,0},{2,1},{3,2},{4,3},{5,4},{6,5},{7,6},{8,7},{9,8},{10,9},{11,1... | collective-permute-start | bytes 3272 | tf_op jit(solution)/shard_map/ppermute | solution.py:20
  22.4 1.9 collective-permute-start.5
  24.5 1.9 collective-permute-start.2
  26.9 0.8 subtract_divide_fusion.3
  27.8 0.8 subtract_divide_fusion.2
  28.6 0.8 subtract_divide_fusion.1
  30.3 0.8 multiply_subtract_fusion
  31.1 0.8 collective-permute-done.5
  31.9 3.5 collective-permute-done.2
  42.3 0.9 fusion.4
  43.2 26.5 %all-gather.5 = f32[128,32,1]{2,0,1:T(8,128)S(1)} all-gather(f32[8,32,1]{2,0,1:T(8,128)S(1)} %get-tuple-element.263), channel_id=7, replica_groups=mesh['lat'=32,'lon'=16] {'lon'}, dimensions={0}, use_global_device_ids=true | all-gather | bytes 17408 | tf_op jit(solution)/shard_map/all_gather | solution.py:123
  69.7 1.4 copy-done
  71.1 24.5 %all-gather.6 = f32[128,32,1]{2,0,1:T(8,128)S(1)} all-gather(f32[8,32,1]{2,0,1:T(8,128)S(1)} %bitcast.111), channel_id=8, replica_groups=mesh['lat'=32,'lon'=16] {'lon'}, dimensions={0}, use_global_device_ids=true | all-gather | bytes 17408 | tf_op jit(solution)/shard_map/all_gather | solution.py:122
  95.6 1.4 copy-done.1
  97.0 23.1 %all-gather.2 = f32[128,32,1]{2,0,1:T(8,128)S(1)} all-gather(f32[8,32,1]{2,0,1:T(8,128)S(1)} %get-tuple-element.153), channel_id=4, replica_groups=mesh['lat'=32,'lon'=16] {'lon'}, dimensions={0}, use_global_device_ids=true | all-gather | bytes 17408 | tf_op jit(solution)/shard_map/all_gather | solution.py:121
  120.7 1.5 slice.1276
  123.0 1.4 copy.162
  124.4 22.4 %all-gather.4 = f32[128,32,1]{2,0,1:T(8,128)S(1)} all-gather(f32[8,32,1]{2,0,1:T(8,128)S(1)} %get-tuple-element.140), channel_id=6, replica_groups=mesh['lat'=32,'lon'=16] {'lon'}, dimensions={0}, use_global_device_ids=true | all-gather | bytes 17408 | tf_op jit(solution)/shard_map/all_gather | solution.py:119
  146.8 1.1 copy.161
  148.0 25.6 %all-gather.1 = f32[128,32,1]{2,0,1:T(8,128)} all-gather(f32[8,32,1]{2,0,1:T(8,128)S(1)} %get-tuple-element.142), channel_id=3, replica_groups=mesh['lat'=32,'lon'=16] {'lon'}, dimensions={0}, use_global_device_ids=true | all-gather | bytes 17408 | tf_op jit(solution)/shard_map/all_gather | solution.py:120
  173.6 2.6 copy.157
  176.4 1.4 copy.166
  178.0 2.9 copy.158
  180.9 24.9 %all-gather = f32[128,32,1]{2,0,1:T(8,128)S(1)} all-gather(f32[8,32,1]{2,0,1:T(8,128)S(1)} %get-tuple-element.143), channel_id=2, replica_groups=mesh['lat'=32,'lon'=16] {'lon'}, dimensions={0}, use_global_device_ids=true | all-gather | bytes 17408 | tf_op jit(solution)/shard_map/all_gather | solution.py:118
  205.8 1.1 copy.156
  206.9 0.9 fusion.40
  209.8 29.7 %all-gather.3 = f32[128,32,1]{2,0,1:T(8,128)S(1)} all-gather(f32[8,32,1]{2,0,1:T(8,128)} %get-tuple-element.141), channel_id=5, replica_groups=mesh['lat'=32,'lon'=16] {'lon'}, dimensions={0}, use_global_device_ids=true | all-gather | bytes 17408 | tf_op jit(solution)/shard_map/all_gather | solution.py:117
  239.4 2.2 fusion.84
  243.2 2.3 copy.165
  245.5 1.0 copy.164
  246.5 1.8 copy.160
  248.3 1.1 copy.169
  249.4 2.3 copy.168
  255.8 0.8 fusion.63
  256.6 61.4 %all-gather.12 = f32[256,1,128]{2,0,1:T(8,128)S(1)} all-gather(f32[8,1,128]{2,0,1:T(8,128)S(1)} %get-tuple-element.238), channel_id=14, replica_groups=mesh['lat'=32,'lon'=16] {'lat'}, dimensions={0}, use_global_device_ids=true | all-gather | bytes 135168 | tf_op jit(solution)/shard_map/all_gather | solution.py:136
  318.0 27.5 %all-gather.11 = f32[256,1,128]{2,0,1:T(8,128)S(1)} all-gather(f32[8,1,128]{2,0,1:T(8,128)S(1)} %get-tuple-element.148), channel_id=13, replica_groups=mesh['lat'=32,'lon'=16] {'lat'}, dimensions={0}, use_global_device_ids=true | all-gather | bytes 135168 | tf_op jit(solution)/shard_map/all_gather | solution.py:132
  345.5 28.8 %all-gather.8 = f32[256,1,128]{2,0,1:T(8,128)S(1)} all-gather(f32[8,1,128]{2,0,1:T(8,128)S(1)} %get-tuple-element.150), channel_id=10, replica_groups=mesh['lat'=32,'lon'=16] {'lat'}, dimensions={0}, use_global_device_ids=true | all-gather | bytes 135168 | tf_op jit(solution)/shard_map/all_gather | solution.py:133
  374.9 6.3 %all-to-all-start = ((f32[32,1,8,128]{3,2,1,0:T(8,128)}), f32[32,1,8,128]{3,2,1,0:T(8,128)S(1)}, u32[]{:S(2)}, u32[]{:S(2)}) async-start(f32[32,1,8,128]{3,2,1,0:T(8,128)} %stack.40), calls=%async_computation | async-start | bytes 262144 | tf_op jit(solution)/shard_map/all_to_all | solution.py:9
  381.2 33.2 %all-gather.9 = f32[256,1,128]{2,0,1:T(8,128)S(1)} all-gather(f32[8,1,128]{2,0,1:T(8,128)S(1)} %get-tuple-element.152), channel_id=11, replica_groups=mesh['lat'=32,'lon'=16] {'lat'}, dimensions={0}, use_global_device_ids=true | all-gather | bytes 135168 | tf_op jit(solution)/shard_map/all_gather | solution.py:134
  414.4 27.9 %all-gather.10 = f32[256,1,128]{2,0,1:T(8,128)S(1)} all-gather(f32[8,1,128]{2,0,1:T(8,128)S(1)} %get-tuple-element.149), channel_id=12, replica_groups=mesh['lat'=32,'lon'=16] {'lat'}, dimensions={0}, use_global_device_ids=true | all-gather | bytes 135168 | tf_op jit(solution)/shard_map/all_gather | solution.py:130
  442.4 29.5 %all-gather.7 = f32[256,1,128]{2,0,1:T(8,128)S(1)} all-gather(f32[8,1,128]{2,0,1:T(8,128)S(1)} %get-tuple-element.151), channel_id=9, replica_groups=mesh['lat'=32,'lon'=16] {'lat'}, dimensions={0}, use_global_device_ids=true | all-gather | bytes 135168 | tf_op jit(solution)/shard_map/all_gather | solution.py:131
  (273 shorter events, 21.5 us)
Async XLA Ops:
  0.9 25.5 %collective-permute-start.7 = (f32[8,1,128]{2,0,1:T(8,128)S(1)}, f32[8,1,128]{2,0,1:T(8,128)S(1)}, u32[]{:S(2)}, u32[]{:S(2)}) collective-permute-start(f32[8,1,128]{2,0,1:T(8,128)S(1)} %slice.1344), channel_id=1, source_target_pairs={{0,16},{16,32},{32,48},{48,64},{64,80},{80,96},{96,112},{112,128},... | collective-permute-start | bytes 12296 | tf_op jit(solution)/shard_map/ppermute | solution.py:19
  4.9 10.5 %collective-permute-start.3 = (f32[8,1,128]{2,0,1:T(8,128)S(1)}, f32[8,1,128]{2,0,1:T(8,128)S(1)}, u32[]{:S(2)}, u32[]{:S(2)}) collective-permute-start(f32[8,1,128]{2,0,1:T(8,128)S(1)} %get-tuple-element.297), channel_id=1, source_target_pairs={{0,16},{16,32},{32,48},{48,64},{64,80},{80,96},{96,112},{112,128},... | collective-permute-start | bytes 12296 | tf_op jit(solution)/shard_map/ppermute | solution.py:19
  4.9 10.5 %collective-permute-start.4 = (f32[8,1,128]{2,0,1:T(8,128)S(1)}, f32[8,1,128]{2,0,1:T(8,128)S(1)}, u32[]{:S(2)}, u32[]{:S(2)}) collective-permute-start(f32[8,1,128]{2,0,1:T(8,128)S(1)} %get-tuple-element.296), channel_id=1, source_target_pairs={{16,0},{32,16},{48,32},{64,48},{80,64},{96,80},{112,96},{128,112},... | collective-permute-start | bytes 12296 | tf_op jit(solution)/shard_map/ppermute | solution.py:20
  9.7 14.7 %collective-permute-start.1 = (f32[8,1,128]{2,0,1:T(8,128)S(1)}, f32[8,1,128]{2,0,1:T(8,128)S(1)}, u32[]{:S(2)}, u32[]{:S(2)}) collective-permute-start(f32[8,1,128]{2,0,1:T(8,128)S(1)} %get-tuple-element.295), channel_id=1, source_target_pairs={{16,0},{32,16},{48,32},{64,48},{80,64},{96,80},{112,96},{128,112},... | collective-permute-start | bytes 12296 | tf_op jit(solution)/shard_map/ppermute | solution.py:20
  13.3 11.1 %collective-permute-start = (f32[8,1,128]{2,0,1:T(8,128)S(1)}, f32[8,1,128]{2,0,1:T(8,128)S(1)}, u32[]{:S(2)}, u32[]{:S(2)}) collective-permute-start(f32[8,1,128]{2,0,1:T(8,128)S(1)} %get-tuple-element.294), channel_id=1, source_target_pairs={{0,16},{16,32},{32,48},{48,64},{64,80},{80,96},{96,112},{112,128},... | collective-permute-start | bytes 12296 | tf_op jit(solution)/shard_map/ppermute | solution.py:19
  15.6 15.5 %collective-permute-start.6 = (f32[8,34,1]{2,0,1:T(8,128)S(1)}, f32[8,34,1]{2,0,1:T(8,128)S(1)}, u32[]{:S(2)}, u32[]{:S(2)}) collective-permute-start(f32[8,34,1]{2,0,1:T(8,128)S(1)} %get-tuple-element.145), channel_id=1, source_target_pairs={{1,0},{2,1},{3,2},{4,3},{5,4},{6,5},{7,6},{8,7},{9,8},{10,9},{11,1... | collective-permute-start | bytes 3272 | tf_op jit(solution)/shard_map/ppermute | solution.py:20
  22.4 9.5 %collective-permute-start.5 = (f32[8,34,1]{2,0,1:T(8,128)S(1)}, f32[8,34,1]{2,0,1:T(8,128)S(1)}, u32[]{:S(2)}, u32[]{:S(2)}) collective-permute-start(f32[8,34,1]{2,0,1:T(8,128)S(1)} %get-tuple-element.144), channel_id=1, source_target_pairs={{0,1},{1,2},{2,3},{3,4},{4,5},{5,6},{6,7},{7,8},{8,9},{9,10},{10,1... | collective-permute-start | bytes 3272 | tf_op jit(solution)/shard_map/ppermute | solution.py:19
  24.5 10.9 %collective-permute-start.2 = (f32[8,34,1]{2,0,1:T(8,128)S(1)}, f32[8,34,1]{2,0,1:T(8,128)S(1)}, u32[]{:S(2)}, u32[]{:S(2)}) collective-permute-start(f32[8,34,1]{2,0,1:T(8,128)S(1)} %pad_maximum_fusion.11), channel_id=1, source_target_pairs={{0,1},{1,2},{2,3},{3,4},{4,5},{5,6},{6,7},{7,8},{8,9},{9,10},{10,1... | collective-permute-start | bytes 3272 | tf_op jit(solution)/shard_map/ppermute | solution.py:19
  42.3 0.9 copy-start.3
  42.3 28.8 %copy-start.4 = (f32[8,32,128]{2,0,1:T(8,128)}, f32[8,32,128]{2,0,1:T(8,128)S(1)}, u32[]{:S(2)}) copy-start(f32[8,32,128]{2,0,1:T(8,128)S(1)} %get-tuple-element.121) | copy-start | bytes 393220
  69.7 1.4 copy-start
  95.6 1.4 copy-start.1
  120.0 2.2 slice-start
  120.7 2.3 slice-start.1
  148.0 28.3 %slice-start.2 = ((f32[128,32,1]{2,0,1:T(8,128)}), f32[8,32,1]{2,0,1:T(8,128)S(1)}, s32[]{:S(2)}) async-start(f32[128,32,1]{2,0,1:T(8,128)} %copy-done.1), calls=%async_computation.3 | async-start | bytes 262144 | tf_op jit(solution)/shard_map/jit(_roll_static)/slice | solution.py:105
  148.0 28.4 %slice-start.3 = ((f32[128,32,1]{2,0,1:T(8,128)}), f32[120,32,1]{2,0,1:T(8,128)S(1)}, s32[]{:S(2)}) async-start(f32[128,32,1]{2,0,1:T(8,128)} %copy-done.1), calls=%async_computation.4 | async-start | bytes 3932160 | tf_op jit(solution)/shard_map/jit(_roll_static)/slice | solution.py:105
  173.6 4.2 copy-start.10
  248.3 3.4 copy-start.2
  248.3 3.4 copy-start.18
  248.3 3.4 copy-start.21
  248.3 3.4 copy-start.22
  248.3 3.4 copy-start.23
  248.3 3.4 copy-start.24
  252.1 0.6 copy-start.26
  252.1 0.7 copy-start.25
  252.4 0.9 copy-start.11
  252.4 1.0 copy-start.12
  253.4 0.9 copy-start.13
  253.4 1.0 copy-start.14
  253.5 1.0 copy-start.5
  253.6 1.0 copy-start.6
  254.5 0.9 copy-start.7
  254.5 1.0 copy-start.8
  254.6 1.0 copy-start.15
  254.6 1.0 copy-start.16
  254.7 1.0 copy-start.17
  374.9 97.0 %all-to-all-start = ((f32[32,1,8,128]{3,2,1,0:T(8,128)}), f32[32,1,8,128]{3,2,1,0:T(8,128)S(1)}, u32[]{:S(2)}, u32[]{:S(2)}) async-start(f32[32,1,8,128]{3,2,1,0:T(8,128)} %stack.40), calls=%async_computation | async-start | bytes 262144 | tf_op jit(solution)/shard_map/all_to_all | solution.py:9
  473.1 0.9 copy-start.9
  473.1 0.9 copy-start.19
  473.1 0.9 copy-start.20
